TPU v7x, 512 devices: a whole 4x4x16 slice. The times are simulated.
512 devices in a mesh: sub: 128 (over y, z, core), case: 4 (over x).
Axes of the slice: x: 4, y: 4, z: 16, core: 2. Of those that a mesh axis runs over, the one named last changes fastest.
Arguments:
- load_interior: float32 [128, 128, 4096], P('sub', None, 'case'), may hold values from -6 to 6
- load_boundary: float32 [128, 128, 1024], P('sub', None, 'case'), may hold values from -6 to 6
- cond_blocks: float32 [128, 128, 4096], P('sub', 'case'), may hold values from -0.25 to 0.25
- block_rows: int32 [128, 128], P('sub', 'case'), may hold values from 0 to 15
- block_cols: int32 [128, 128], P('sub', 'case'), may hold values from 0 to 63, as said below
- interface_maps: int32 [128, 7, 2, 1024], P('sub'), may hold values from 0 to 1023, as said below
- merge_maps: float32 [128, 7, 1024, 512], P('sub', None, 'case'), as said below
Outputs:
- leaf_loads: float32 [128, 1024, 128], P('sub', 'case')
- node_loads: float32 [128, 1024, 128], P('sub', 'case')
Inputs may be any that keep to these rules, and one draw needn't show every extreme that they name: `block_cols`: entry k of a substructure's row lies in [(k // 32) * 16, (k // 32 + 1) * 16); blocks may repeat. `interface_maps`: each row of 1024 entries is a permutation; at level index l, slots that agree in all but their lowest l + 1 bits hold equal entries. `merge_maps`: at level index l, slots that agree in all but their lowest l + 1 bits hold equal entries.
All inputs are finite; a program needn't handle non-finite values.
Results may differ from a plain program's by a relative error of at most 0.0003.
Values sent between devices are 32-bit elements; how exact they have to be, the bound alone decides.
No kernel may reach another device: no remote copies, remote signals or barrier semaphores. Data moves between devices by JAX's collectives and lax.ppermute only.
A program may use at most 64 MiB of HBM per device.

v0:
```python
import jax
import jax.numpy as jnp
from jax import lax
from jax.sharding import PartitionSpec as P

BLK = 64


def from_partner(value, axis, distance):
    mask = 2**distance
    pairs = [(source, source ^ mask) for source in range(lax.axis_size(axis))]
    return lax.ppermute(value, axis, pairs)


def on_device(
    load_interior, load_boundary, cond_blocks, block_rows, block_cols, interface_maps, merge_maps
):
    interior, boundary = (
        lax.all_to_all(load_interior, "sub", split_axis=1, concat_axis=0, tiled=True),
        lax.all_to_all(load_boundary, "sub", split_axis=1, concat_axis=0, tiled=True),
    )
    interior = jnp.transpose(interior[:, 0, :])
    boundary = jnp.transpose(boundary[:, 0, :])
    local_rows = interior.shape[0]
    num_cases = interior.shape[1]
    block_count = cond_blocks.shape[1]
    block_size = BLK
    blocks = cond_blocks[0].reshape(block_count, block_size, block_size)
    quarter = boundary.shape[0]
    groups = lax.axis_size("case")
    full_rows = quarter * groups
    position = lax.axis_index("case")
    local_cols = block_cols[0] - position * (local_rows // block_size)
    pieces = jnp.take(
        interior.reshape(local_rows // block_size, block_size, num_cases), local_cols, axis=0
    )
    products = jnp.einsum("krc,kcn->krn", blocks, pieces, precision=lax.Precision.HIGHEST)
    row_blocks = full_rows // block_size
    onehot = (block_rows[0][None, :] == jnp.arange(row_blocks, dtype=jnp.int32)[:, None]).astype(
        jnp.float32
    )
    partial_value = jnp.dot(
        onehot,
        products.reshape(block_count, block_size * num_cases),
        precision=lax.Precision.HIGHEST,
    )
    partial_value = partial_value.reshape(full_rows, num_cases)
    embedded = lax.dynamic_update_slice(
        jnp.zeros((full_rows, num_cases), jnp.float32), boundary, (position * quarter, 0)
    )
    contribution = embedded - partial_value
    current = lax.psum(contribution, "case")
    leaf_share = lax.dynamic_slice_in_dim(current, position * quarter, quarter, 0)
    slot = lax.axis_index("sub")
    levels = lax.axis_size("sub").bit_length() - 1
    nodes = jnp.zeros((quarter, num_cases), jnp.float32)
    for level in range(1, levels + 1):
        half = 1 << level - 1
        maps = interface_maps[0, level - 1]
        matrix = merge_maps[0, level - 1]
        shared_rows = matrix.shape[1]
        kept_index = jnp.concatenate([maps[0, shared_rows:], maps[1, shared_rows:] + full_rows])
        mine = lax.dynamic_slice_in_dim(kept_index, position * quarter, quarter)
        other = from_partner(current, "sub", level - 1)
        own_full, other_full = (current, other)
        upper = slot // half % 2 == 1
        left_full = jnp.where(upper, other_full, own_full)
        right_full = jnp.where(upper, own_full, other_full)
        stacked = jnp.concatenate([left_full, right_full], axis=0)
        shared = jnp.take(stacked, maps[0, :shared_rows], axis=0) + jnp.take(
            stacked, maps[1, :shared_rows] + full_rows, axis=0
        )
        parent = jnp.take(stacked, mine, axis=0) - jnp.dot(
            matrix, shared, precision=lax.Precision.HIGHEST
        )
        is_node = slot % (2 * half) == half
        if level == levels:
            is_node = jnp.logical_or(is_node, slot == 0)
        nodes = jnp.where(is_node, parent, nodes)
        if level < levels:
            current = lax.all_gather(parent, "case", axis=0, tiled=True)
    return (leaf_share[None], nodes[None])


def solution(mesh):
    placed = (
        P("sub", None, "case"),
        P("sub", None, "case"),
        P("sub", "case", None),
        P("sub", "case"),
        P("sub", "case"),
        P("sub", None, None, None),
        P("sub", None, "case", None),
    )
    return jax.shard_map(
        on_device,
        mesh=mesh,
        in_specs=placed,
        out_specs=(P("sub", "case", None), P("sub", "case", None)),
        check_vma=False,
    )
```

profile of v0, /device:TPU:8, one launch (start us, length us, event | category | flops | bytes accessed | tf_op | source)
XLA Modules:
  0.0 423.4 jit_solution(13161478264808261519)
XLA Ops:
  8.9 19.6 %all-to-all-start = ((f32[1,128,256]{2,0,1:T(1,128)}), f32[1,128,256]{2,0,1:T(1,128)S(1)}, u32[]{:S(2)}, u32[]{:S(2)}) async-start(f32[1,128,256]{2,0,1:T(1,128)} %copy.64), calls=%async_computation | async-start | bytes 262144 | tf_op jit(solution)/shard_map/all_to_all | solution.py:20
  28.5 2.4 copy.66
  32.8 12.9 %all-to-all-done = f32[1,128,256]{2,0,1:T(1,128)S(1)} async-done(((f32[1,128,256]{2,0,1:T(1,128)}), f32[1,128,256]{2,0,1:T(1,128)S(1)}, u32[]{:S(2)}, u32[]{:S(2)}) %all-to-all-start) | async-done | bytes 131104 | tf_op jit(solution)/shard_map/all_to_all | solution.py:20
  45.7 7.2 %all-to-all-start.1 = ((f32[1,128,1024]{2,0,1:T(1,128)}), f32[1,128,1024]{2,0,1:T(1,128)S(1)}, u32[]{:S(2)}, u32[]{:S(2)}) async-start(f32[1,128,1024]{2,0,1:T(1,128)} %copy.66), calls=%async_computation.1 | async-start | bytes 1048576 | tf_op jit(solution)/shard_map/all_to_all | solution.py:19
  55.1 31.4 %all-to-all-done.1 = f32[1,128,1024]{2,0,1:T(1,128)S(1)} async-done(((f32[1,128,1024]{2,0,1:T(1,128)}), f32[1,128,1024]{2,0,1:T(1,128)S(1)}, u32[]{:S(2)}, u32[]{:S(2)}) %all-to-all-start.1) | async-done | bytes 524320 | tf_op jit(solution)/shard_map/all_to_all | solution.py:19
  90.9 50.0 %all-reduce.2.cloned.1.call-done = f32[1024,128]{1,0:T(8,128)} async-done(((f32[1024,128]{1,0:T(8,128)}), f32[1024,128]{1,0:T(8,128)}) %all-reduce.2.cloned.1.call-update) | async-done | bytes 524304 | tf_op jit(solution)/shard_map/psum | solution.py:52
  150.9 12.8 %all_gather.18 = f32[1024,128]{0,1:T(8,128)S(1)} all-gather(f32[256,128]{0,1:T(8,128)S(1)} %fusion.8), channel_id=1, replica_groups=mesh['sub'=128,'case'=4] {'case'}, dimensions={0}, use_global_device_ids=true | all-gather | bytes 655360 | tf_op jit(solution)/shard_map/all_gather | solution.py:81
  163.6 3.6 collective-permute-start.1
  167.4 9.3 %collective-permute-done.1 = f32[1024,128]{0,1:T(8,128)S(1)} collective-permute-done((f32[1024,128]{0,1:T(8,128)S(1)}, f32[1024,128]{0,1:T(8,128)S(1)}, u32[]{:S(2)}, u32[]{:S(2)}) %collective-permute-start.1) | collective-permute-done | bytes 524320 | tf_op jit(solution)/shard_map/ppermute | solution.py:12
  182.0 13.1 %all_gather.19 = f32[1024,128]{0,1:T(8,128)S(1)} all-gather(f32[256,128]{0,1:T(8,128)S(1)} %fusion.7), channel_id=1, replica_groups=mesh['sub'=128,'case'=4] {'case'}, dimensions={0}, use_global_device_ids=true | all-gather | bytes 655360 | tf_op jit(solution)/shard_map/all_gather | solution.py:81
  195.1 4.4 %collective-permute-start.2 = (f32[1024,128]{0,1:T(8,128)S(1)}, f32[1024,128]{0,1:T(8,128)S(1)}, u32[]{:S(2)}, u32[]{:S(2)}) collective-permute-start(f32[1024,128]{0,1:T(8,128)S(1)} %all_gather.19), channel_id=1, source_target_pairs={{0,16},{4,20},{8,24},{12,28},{16,0},{20,4},{24,8},{28,12},{32,48},... | collective-permute-start | bytes 1572872 | tf_op jit(solution)/shard_map/ppermute | solution.py:12
  199.6 16.8 %collective-permute-done.2 = f32[1024,128]{0,1:T(8,128)S(1)} collective-permute-done((f32[1024,128]{0,1:T(8,128)S(1)}, f32[1024,128]{0,1:T(8,128)S(1)}, u32[]{:S(2)}, u32[]{:S(2)}) %collective-permute-start.2) | collective-permute-done | bytes 524320 | tf_op jit(solution)/shard_map/ppermute | solution.py:12
  221.8 13.3 %all_gather.20 = f32[1024,128]{0,1:T(8,128)S(1)} all-gather(f32[256,128]{0,1:T(8,128)S(1)} %fusion.6), channel_id=1, replica_groups=mesh['sub'=128,'case'=4] {'case'}, dimensions={0}, use_global_device_ids=true | all-gather | bytes 655360 | tf_op jit(solution)/shard_map/all_gather | solution.py:81
  235.1 7.6 %collective-permute-start.3 = (f32[1024,128]{0,1:T(8,128)S(1)}, f32[1024,128]{0,1:T(8,128)S(1)}, u32[]{:S(2)}, u32[]{:S(2)}) collective-permute-start(f32[1024,128]{0,1:T(8,128)S(1)} %all_gather.20), channel_id=1, source_target_pairs={{0,32},{4,36},{8,40},{12,44},{16,48},{20,52},{24,56},{28,60},{32,0... | collective-permute-start | bytes 1572872 | tf_op jit(solution)/shard_map/ppermute | solution.py:12
  242.8 40.0 %collective-permute-done.3 = f32[1024,128]{0,1:T(8,128)S(1)} collective-permute-done((f32[1024,128]{0,1:T(8,128)S(1)}, f32[1024,128]{0,1:T(8,128)S(1)}, u32[]{:S(2)}, u32[]{:S(2)}) %collective-permute-start.3) | collective-permute-done | bytes 524320 | tf_op jit(solution)/shard_map/ppermute | solution.py:12
  288.1 12.8 %all_gather.21 = f32[1024,128]{0,1:T(8,128)S(1)} all-gather(f32[256,128]{0,1:T(8,128)S(1)} %fusion.5), channel_id=1, replica_groups=mesh['sub'=128,'case'=4] {'case'}, dimensions={0}, use_global_device_ids=true | all-gather | bytes 655360 | tf_op jit(solution)/shard_map/all_gather | solution.py:81
  300.9 11.2 %collective-permute-start.4 = (f32[1024,128]{0,1:T(8,128)S(1)}, f32[1024,128]{0,1:T(8,128)S(1)}, u32[]{:S(2)}, u32[]{:S(2)}) collective-permute-start(f32[1024,128]{0,1:T(8,128)S(1)} %all_gather.21), channel_id=1, source_target_pairs={{0,64},{4,68},{8,72},{12,76},{16,80},{20,84},{24,88},{28,92},{32,9... | collective-permute-start | bytes 1572872 | tf_op jit(solution)/shard_map/ppermute | solution.py:12
  312.1 36.2 %collective-permute-done.4 = f32[1024,128]{0,1:T(8,128)S(1)} collective-permute-done((f32[1024,128]{0,1:T(8,128)S(1)}, f32[1024,128]{0,1:T(8,128)S(1)}, u32[]{:S(2)}, u32[]{:S(2)}) %collective-permute-start.4) | collective-permute-done | bytes 524320 | tf_op jit(solution)/shard_map/ppermute | solution.py:12
  353.6 13.2 %all_gather.22 = f32[1024,128]{0,1:T(8,128)S(1)} all-gather(f32[256,128]{0,1:T(8,128)S(1)} %fusion.4), channel_id=1, replica_groups=mesh['sub'=128,'case'=4] {'case'}, dimensions={0}, use_global_device_ids=true | all-gather | bytes 655360 | tf_op jit(solution)/shard_map/all_gather | solution.py:81
  366.8 2.4 collective-permute-start.5
  369.3 10.0 %collective-permute-done.5 = f32[1024,128]{0,1:T(8,128)S(1)} collective-permute-done((f32[1024,128]{0,1:T(8,128)S(1)}, f32[1024,128]{0,1:T(8,128)S(1)}, u32[]{:S(2)}, u32[]{:S(2)}) %collective-permute-start.5) | collective-permute-done | bytes 524320 | tf_op jit(solution)/shard_map/ppermute | solution.py:12
  384.6 13.3 %all_gather.23 = f32[1024,128]{0,1:T(8,128)S(1)} all-gather(f32[256,128]{0,1:T(8,128)S(1)} %fusion.3), channel_id=1, replica_groups=mesh['sub'=128,'case'=4] {'case'}, dimensions={0}, use_global_device_ids=true | all-gather | bytes 655360 | tf_op jit(solution)/shard_map/all_gather | solution.py:81
  397.8 4.0 collective-permute-start.6
  403.5 6.9 %collective-permute-done.6 = f32[1024,128]{0,1:T(8,128)S(1)} collective-permute-done((f32[1024,128]{0,1:T(8,128)S(1)}, f32[1024,128]{0,1:T(8,128)S(1)}, u32[]{:S(2)}, u32[]{:S(2)}) %collective-permute-start.6) | collective-permute-done | bytes 524320 | tf_op jit(solution)/shard_map/ppermute | solution.py:12
  (140 shorter events, 53.6 us)
Async XLA Ops:
  7.2 47.8 %copy-start.1 = (s32[1,32]{1,0:T(1,128)S(1)}, s32[1,32]{1,0:T(1,128)}, u32[]{:S(2)}) copy-start(s32[1,32]{1,0:T(1,128)} %param.15) | copy-start | bytes 388
  8.9 36.8 %all-to-all-start = ((f32[1,128,256]{2,0,1:T(1,128)}), f32[1,128,256]{2,0,1:T(1,128)S(1)}, u32[]{:S(2)}, u32[]{:S(2)}) async-start(f32[1,128,256]{2,0,1:T(1,128)} %copy.64), calls=%async_computation | async-start | bytes 262144 | tf_op jit(solution)/shard_map/all_to_all | solution.py:20
  45.7 40.8 %all-to-all-start.1 = ((f32[1,128,1024]{2,0,1:T(1,128)}), f32[1,128,1024]{2,0,1:T(1,128)S(1)}, u32[]{:S(2)}, u32[]{:S(2)}) async-start(f32[1,128,1024]{2,0,1:T(1,128)} %copy.66), calls=%async_computation.1 | async-start | bytes 1048576 | tf_op jit(solution)/shard_map/all_to_all | solution.py:19
  52.9 87.9 %all-reduce.2.cloned.1.call-start = ((), (), s32[]{:S(2)}) async-start(), calls=%async_computation.2 | async-start | bytes 1048576 | tf_op jit(solution)/shard_map/psum | solution.py:52
  54.9 33.8 %copy-start = (s32[1,32]{1,0:T(1,128)S(1)}, s32[1,32]{1,0:T(1,128)}, u32[]{:S(2)}) copy-start(s32[1,32]{1,0:T(1,128)} %param.14) | copy-start | bytes 388
  140.8 4.0 collective-permute-start
  163.6 13.0 %collective-permute-start.1 = (f32[1024,128]{0,1:T(8,128)S(1)}, f32[1024,128]{0,1:T(8,128)S(1)}, u32[]{:S(2)}, u32[]{:S(2)}) collective-permute-start(f32[1024,128]{0,1:T(8,128)S(1)} %all_gather.18), channel_id=1, source_target_pairs={{0,8},{4,12},{8,0},{12,4},{16,24},{20,28},{24,16},{28,20},{32,40},... | collective-permute-start | bytes 1572872 | tf_op jit(solution)/shard_map/ppermute | solution.py:12
  195.1 21.3 %collective-permute-start.2 = (f32[1024,128]{0,1:T(8,128)S(1)}, f32[1024,128]{0,1:T(8,128)S(1)}, u32[]{:S(2)}, u32[]{:S(2)}) collective-permute-start(f32[1024,128]{0,1:T(8,128)S(1)} %all_gather.19), channel_id=1, source_target_pairs={{0,16},{4,20},{8,24},{12,28},{16,0},{20,4},{24,8},{28,12},{32,48},... | collective-permute-start | bytes 1572872 | tf_op jit(solution)/shard_map/ppermute | solution.py:12
  235.1 47.6 %collective-permute-start.3 = (f32[1024,128]{0,1:T(8,128)S(1)}, f32[1024,128]{0,1:T(8,128)S(1)}, u32[]{:S(2)}, u32[]{:S(2)}) collective-permute-start(f32[1024,128]{0,1:T(8,128)S(1)} %all_gather.20), channel_id=1, source_target_pairs={{0,32},{4,36},{8,40},{12,44},{16,48},{20,52},{24,56},{28,60},{32,0... | collective-permute-start | bytes 1572872 | tf_op jit(solution)/shard_map/ppermute | solution.py:12
  300.9 47.4 %collective-permute-start.4 = (f32[1024,128]{0,1:T(8,128)S(1)}, f32[1024,128]{0,1:T(8,128)S(1)}, u32[]{:S(2)}, u32[]{:S(2)}) collective-permute-start(f32[1024,128]{0,1:T(8,128)S(1)} %all_gather.21), channel_id=1, source_target_pairs={{0,64},{4,68},{8,72},{12,76},{16,80},{20,84},{24,88},{28,92},{32,9... | collective-permute-start | bytes 1572872 | tf_op jit(solution)/shard_map/ppermute | solution.py:12
  366.8 12.5 %collective-permute-start.5 = (f32[1024,128]{0,1:T(8,128)S(1)}, f32[1024,128]{0,1:T(8,128)S(1)}, u32[]{:S(2)}, u32[]{:S(2)}) collective-permute-start(f32[1024,128]{0,1:T(8,128)S(1)} %all_gather.22), channel_id=1, source_target_pairs={{0,128},{4,132},{8,136},{12,140},{16,144},{20,148},{24,152},{28,15... | collective-permute-start | bytes 1572872 | tf_op jit(solution)/shard_map/ppermute | solution.py:12
  397.8 12.6 %collective-permute-start.6 = (f32[1024,128]{0,1:T(8,128)S(1)}, f32[1024,128]{0,1:T(8,128)S(1)}, u32[]{:S(2)}, u32[]{:S(2)}) collective-permute-start(f32[1024,128]{0,1:T(8,128)S(1)} %all_gather.23), channel_id=1, source_target_pairs={{0,256},{4,260},{8,264},{12,268},{16,272},{20,276},{24,280},{28,28... | collective-permute-start | bytes 1572872 | tf_op jit(solution)/shard_map/ppermute | solution.py:12
Sparse Core Ops, SparseCore 0:
  91.0 49.8 all-reduce.1
where the time goes:
time: 424 us; the launch traced here: 423 us
  waiting for transfers between devices  215 us (51%)
  blocking collectives  78.5 us (19%)
  starting transfers between devices  62.1 us (15%)
  local copies, waits for them, and re-layouts  32.1 us (8%)
  matrix products  15.4 us (4%)
  between operations  15.3 us (4%)
  other arithmetic  4.42 us (1%)
    ppermute x7, waiting for transfers between devices, from_partner(): return lax.ppermute(value, axis, pairs)  121 us
    all_gather x6, blocking collectives, on_device(): current = lax.all_gather(parent, 'case', axis=0, tiled=True)  78.5 us
    psum x1, waiting for transfers between devices, on_device(): current = lax.psum(contribution, 'case')  50 us
    ppermute x7, starting transfers between devices, from_partner(): return lax.ppermute(value, axis, pairs)  35.3 us
    all_to_all x1, waiting for transfers between devices, on_device(): lax.all_to_all(load_interior, 'sub', split_axis=1, concat_axis=0, tiled=T...  31.4 us
    all_to_all x1, starting transfers between devices, on_device(): lax.all_to_all(load_boundary, 'sub', split_axis=1, concat_axis=0, tiled=T...  19.6 us
    dot_general x7, matrix products, on_device(): jnp.dot(matrix, shared, precision=lax.Precision.HIGHEST)  13.2 us
    all_to_all x1, waiting for transfers between devices, on_device(): lax.all_to_all(load_boundary, 'sub', split_axis=1, concat_axis=0, tiled=T...  12.9 us
  transfers between devices with their start and end apart: 10, of which 10 were waited for; matrix products, arithmetic and copies ran while one was open for 2% of the time, Pallas kernels for 0%

commit v1 on v0

--- a/solution.py
+++ b/solution.py
@@ -78,7 +78,9 @@
             is_node = jnp.logical_or(is_node, slot == 0)
         nodes = jnp.where(is_node, parent, nodes)
         if level < levels:
-            current = lax.all_gather(parent, "case", axis=0, tiled=True)
+            current = jnp.concatenate(
+                lax.all_to_all(jnp.stack([parent] * lax.axis_size("case")), "case", 0, 0), axis=0
+            )
     return (leaf_share[None], nodes[None])
 
 

time: 424 us -> 439 us (1.035)
  blocking collectives: 78.5 us -> 0 us
  waiting for transfers between devices: 215 us -> 283 us
  starting transfers between devices: 62.1 us -> 83.4 us
    all_gather x6 -> x0, blocking collectives: 78.5 us -> none  [on_device(): current = lax.all_gather(parent, 'case', axis=0, tiled=True)]
    all_to_all x0 -> x6, waiting for transfers between devices: none -> 54.4 us  [on_device(): lax.all_to_all(jnp.stack([parent] * lax.axis_size('case')), 'case', 0, 0)]
    all_to_all x0 -> x6, starting transfers between devices: none -> 21 us  [on_device(): lax.all_to_all(jnp.stack([parent] * lax.axis_size('case')), 'case', 0, 0)]
    ppermute x7, waiting for transfers between devices: 121 us -> 134 us  [from_partner(): return lax.ppermute(value, axis, pairs)]
    another operation x0 -> x6, local copies, waits for them, and re-layouts: none -> 5.14 us  [on_device(): jnp.stack([parent] * lax.axis_size('case'))]
  transfers between devices with their start and end apart: 10 -> 16, of which waited for: 10 -> 16; matrix products, arithmetic and copies ran while one was open for 2% -> 2% of each run, Pallas kernels for 0% -> 0%
where the time goes in v1:
time: 439 us; the launch traced here: 437 us
  waiting for transfers between devices  283 us (64%)
  starting transfers between devices  83.4 us (19%)
  local copies, waits for them, and re-layouts  35.9 us (8%)
  matrix products  15.4 us (4%)
  between operations  15.3 us (3%)
    ppermute x7, waiting for transfers between devices, from_partner(): return lax.ppermute(value, axis, pairs)  134 us
    all_to_all x6, waiting for transfers between devices, on_device(): lax.all_to_all(jnp.stack([parent] * lax.axis_size('case')), 'case', 0, 0)  54.4 us
    psum x1, waiting for transfers between devices, on_device(): current = lax.psum(contribution, 'case')  50 us
    ppermute x7, starting transfers between devices, from_partner(): return lax.ppermute(value, axis, pairs)  35.5 us
    all_to_all x1, waiting for transfers between devices, on_device(): lax.all_to_all(load_interior, 'sub', split_axis=1, concat_axis=0, tiled=T...  33.2 us
    all_to_all x6, starting transfers between devices, on_device(): lax.all_to_all(jnp.stack([parent] * lax.axis_size('case')), 'case', 0, 0)  21 us
    all_to_all x1, starting transfers between devices, on_device(): lax.all_to_all(load_boundary, 'sub', split_axis=1, concat_axis=0, tiled=T...  19.6 us
    dot_general x7, matrix products, on_device(): jnp.dot(matrix, shared, precision=lax.Precision.HIGHEST)  13.2 us
  transfers between devices with their start and end apart: 16, of which 16 were waited for; matrix products, arithmetic and copies ran while one was open for 2% of the time, Pallas kernels for 0%

profile of v1, /device:TPU:8, one launch (start us, length us, event | category | flops | bytes accessed | tf_op | source)
XLA Modules:
  0.0 437.3 jit_solution(12870179634023051125)
XLA Ops:
  8.9 19.6 %all-to-all-start = ((f32[1,128,256]{2,0,1:T(1,128)}), f32[1,128,256]{2,0,1:T(1,128)S(1)}, u32[]{:S(2)}, u32[]{:S(2)}) async-start(f32[1,128,256]{2,0,1:T(1,128)} %copy.40), calls=%async_computation | async-start | bytes 262144 | tf_op jit(solution)/shard_map/all_to_all | solution.py:20
  34.1 11.6 %all-to-all-done = f32[1,128,256]{2,0,1:T(1,128)S(1)} async-done(((f32[1,128,256]{2,0,1:T(1,128)}), f32[1,128,256]{2,0,1:T(1,128)S(1)}, u32[]{:S(2)}, u32[]{:S(2)}) %all-to-all-start) | async-done | bytes 131104 | tf_op jit(solution)/shard_map/all_to_all | solution.py:20
  45.7 7.2 %all-to-all-start.1 = ((f32[1,128,1024]{2,0,1:T(1,128)}), f32[1,128,1024]{2,0,1:T(1,128)S(1)}, u32[]{:S(2)}, u32[]{:S(2)}) async-start(f32[1,128,1024]{2,0,1:T(1,128)} %copy.42), calls=%async_computation.1 | async-start | bytes 1048576 | tf_op jit(solution)/shard_map/all_to_all | solution.py:19
  53.4 33.2 %all-to-all-done.1 = f32[1,128,1024]{2,0,1:T(1,128)S(1)} async-done(((f32[1,128,1024]{2,0,1:T(1,128)}), f32[1,128,1024]{2,0,1:T(1,128)S(1)}, u32[]{:S(2)}, u32[]{:S(2)}) %all-to-all-start.1) | async-done | bytes 524320 | tf_op jit(solution)/shard_map/all_to_all | solution.py:19
  90.9 50.0 %all-reduce.2.cloned.1.call-done = f32[1024,128]{1,0:T(8,128)} async-done(((f32[1024,128]{1,0:T(8,128)}), f32[1024,128]{1,0:T(8,128)}) %all-reduce.2.cloned.1.call-update) | async-done | bytes 524304 | tf_op jit(solution)/shard_map/psum | solution.py:52
  151.8 3.6 all-to-all-start.2
  155.5 9.8 %all-to-all-done.2 = f32[4,256,128]{2,1,0:T(8,128)S(1)} async-done(((f32[4,256,128]{2,1,0:T(8,128)}), f32[4,256,128]{2,1,0:T(8,128)S(1)}, u32[]{:S(2)}, u32[]{:S(2)}) %all-to-all-start.2) | async-done | bytes 524320 | tf_op jit(solution)/shard_map/all_to_all | solution.py:82
  165.3 3.6 collective-permute-start.1
  169.0 11.1 %collective-permute-done.1 = f32[1024,128]{1,0:T(8,128)S(1)} collective-permute-done((f32[1024,128]{1,0:T(8,128)S(1)}, f32[1024,128]{1,0:T(8,128)S(1)}, u32[]{:S(2)}, u32[]{:S(2)}) %collective-permute-start.1) | collective-permute-done | bytes 524320 | tf_op jit(solution)/shard_map/ppermute | solution.py:12
  186.0 3.5 all-to-all-start.3
  189.5 8.0 %all-to-all-done.3 = f32[4,256,128]{2,1,0:T(8,128)S(1)} async-done(((f32[4,256,128]{2,1,0:T(8,128)}), f32[4,256,128]{2,1,0:T(8,128)S(1)}, u32[]{:S(2)}, u32[]{:S(2)}) %all-to-all-start.3) | async-done | bytes 524320 | tf_op jit(solution)/shard_map/all_to_all | solution.py:82
  197.5 4.5 %collective-permute-start.2 = (f32[1024,128]{1,0:T(8,128)S(1)}, f32[1024,128]{1,0:T(8,128)S(1)}, u32[]{:S(2)}, u32[]{:S(2)}) collective-permute-start(f32[1024,128]{1,0:T(8,128)S(1)} %bitcast.142), channel_id=1, source_target_pairs={{0,16},{4,20},{8,24},{12,28},{16,0},{20,4},{24,8},{28,12},{32,48},... | collective-permute-start | bytes 1572872 | tf_op jit(solution)/shard_map/ppermute | solution.py:12
  202.1 20.3 %collective-permute-done.2 = f32[1024,128]{1,0:T(8,128)S(1)} collective-permute-done((f32[1024,128]{1,0:T(8,128)S(1)}, f32[1024,128]{1,0:T(8,128)S(1)}, u32[]{:S(2)}, u32[]{:S(2)}) %collective-permute-start.2) | collective-permute-done | bytes 524320 | tf_op jit(solution)/shard_map/ppermute | solution.py:12
  231.8 8.8 %all-to-all-done.4 = f32[4,256,128]{2,1,0:T(8,128)S(1)} async-done(((f32[4,256,128]{2,1,0:T(8,128)}), f32[4,256,128]{2,1,0:T(8,128)S(1)}, u32[]{:S(2)}, u32[]{:S(2)}) %all-to-all-start.4) | async-done | bytes 524320 | tf_op jit(solution)/shard_map/all_to_all | solution.py:82
  240.6 7.6 %collective-permute-start.3 = (f32[1024,128]{1,0:T(8,128)S(1)}, f32[1024,128]{1,0:T(8,128)S(1)}, u32[]{:S(2)}, u32[]{:S(2)}) collective-permute-start(f32[1024,128]{1,0:T(8,128)S(1)} %bitcast.146), channel_id=1, source_target_pairs={{0,32},{4,36},{8,40},{12,44},{16,48},{20,52},{24,56},{28,60},{32,0... | collective-permute-start | bytes 1572872 | tf_op jit(solution)/shard_map/ppermute | solution.py:12
  248.4 42.4 %collective-permute-done.3 = f32[1024,128]{1,0:T(8,128)S(1)} collective-permute-done((f32[1024,128]{1,0:T(8,128)S(1)}, f32[1024,128]{1,0:T(8,128)S(1)}, u32[]{:S(2)}, u32[]{:S(2)}) %collective-permute-start.3) | collective-permute-done | bytes 524320 | tf_op jit(solution)/shard_map/ppermute | solution.py:12
  300.2 9.9 %all-to-all-done.5 = f32[4,256,128]{2,1,0:T(8,128)S(1)} async-done(((f32[4,256,128]{2,1,0:T(8,128)}), f32[4,256,128]{2,1,0:T(8,128)S(1)}, u32[]{:S(2)}, u32[]{:S(2)}) %all-to-all-start.5) | async-done | bytes 524320 | tf_op jit(solution)/shard_map/all_to_all | solution.py:82
  310.1 11.5 %collective-permute-start.4 = (f32[1024,128]{1,0:T(8,128)S(1)}, f32[1024,128]{1,0:T(8,128)S(1)}, u32[]{:S(2)}, u32[]{:S(2)}) collective-permute-start(f32[1024,128]{1,0:T(8,128)S(1)} %bitcast.144), channel_id=1, source_target_pairs={{0,64},{4,68},{8,72},{12,76},{16,80},{20,84},{24,88},{28,92},{32,9... | collective-permute-start | bytes 1572872 | tf_op jit(solution)/shard_map/ppermute | solution.py:12
  321.7 37.1 %collective-permute-done.4 = f32[1024,128]{1,0:T(8,128)S(1)} collective-permute-done((f32[1024,128]{1,0:T(8,128)S(1)}, f32[1024,128]{1,0:T(8,128)S(1)}, u32[]{:S(2)}, u32[]{:S(2)}) %collective-permute-start.4) | collective-permute-done | bytes 524320 | tf_op jit(solution)/shard_map/ppermute | solution.py:12
  368.2 9.9 %all-to-all-done.6 = f32[4,256,128]{2,1,0:T(8,128)S(1)} async-done(((f32[4,256,128]{2,1,0:T(8,128)}), f32[4,256,128]{2,1,0:T(8,128)S(1)}, u32[]{:S(2)}, u32[]{:S(2)}) %all-to-all-start.6) | async-done | bytes 524320 | tf_op jit(solution)/shard_map/all_to_all | solution.py:82
  380.6 12.4 %collective-permute-done.5 = f32[1024,128]{1,0:T(8,128)S(1)} collective-permute-done((f32[1024,128]{1,0:T(8,128)S(1)}, f32[1024,128]{1,0:T(8,128)S(1)}, u32[]{:S(2)}, u32[]{:S(2)}) %collective-permute-start.5) | collective-permute-done | bytes 524320 | tf_op jit(solution)/shard_map/ppermute | solution.py:12
  402.5 8.0 %all-to-all-done.7 = f32[4,256,128]{2,1,0:T(8,128)S(1)} async-done(((f32[4,256,128]{2,1,0:T(8,128)}), f32[4,256,128]{2,1,0:T(8,128)S(1)}, u32[]{:S(2)}, u32[]{:S(2)}) %all-to-all-start.7) | async-done | bytes 524320 | tf_op jit(solution)/shard_map/all_to_all | solution.py:82
  410.5 3.9 collective-permute-start.6
  416.0 8.7 %collective-permute-done.6 = f32[1024,128]{1,0:T(8,128)S(1)} collective-permute-done((f32[1024,128]{1,0:T(8,128)S(1)}, f32[1024,128]{1,0:T(8,128)S(1)}, u32[]{:S(2)}, u32[]{:S(2)}) %collective-permute-start.6) | collective-permute-done | bytes 524320 | tf_op jit(solution)/shard_map/ppermute | solution.py:12
  (152 shorter events, 75.9 us)
Async XLA Ops:
  7.2 46.0 %copy-start.1 = (s32[1,32]{1,0:T(1,128)S(1)}, s32[1,32]{1,0:T(1,128)}, u32[]{:S(2)}) copy-start(s32[1,32]{1,0:T(1,128)} %param.15) | copy-start | bytes 388
  8.9 36.8 %all-to-all-start = ((f32[1,128,256]{2,0,1:T(1,128)}), f32[1,128,256]{2,0,1:T(1,128)S(1)}, u32[]{:S(2)}, u32[]{:S(2)}) async-start(f32[1,128,256]{2,0,1:T(1,128)} %copy.40), calls=%async_computation | async-start | bytes 262144 | tf_op jit(solution)/shard_map/all_to_all | solution.py:20
  45.7 40.9 %all-to-all-start.1 = ((f32[1,128,1024]{2,0,1:T(1,128)}), f32[1,128,1024]{2,0,1:T(1,128)S(1)}, u32[]{:S(2)}, u32[]{:S(2)}) async-start(f32[1,128,1024]{2,0,1:T(1,128)} %copy.42), calls=%async_computation.1 | async-start | bytes 1048576 | tf_op jit(solution)/shard_map/all_to_all | solution.py:19
  52.9 87.9 %all-reduce.2.cloned.1.call-start = ((), (), s32[]{:S(2)}) async-start(), calls=%async_computation.8 | async-start | bytes 1048576 | tf_op jit(solution)/shard_map/psum | solution.py:52
  53.2 35.6 %copy-start = (s32[1,32]{1,0:T(1,128)S(1)}, s32[1,32]{1,0:T(1,128)}, u32[]{:S(2)}) copy-start(s32[1,32]{1,0:T(1,128)} %param.14) | copy-start | bytes 388
  140.9 4.0 collective-permute-start
  151.8 13.5 %all-to-all-start.2 = ((f32[4,256,128]{2,1,0:T(8,128)}), f32[4,256,128]{2,1,0:T(8,128)S(1)}, u32[]{:S(2)}, u32[]{:S(2)}) async-start(f32[4,256,128]{2,1,0:T(8,128)} %stack.12), calls=%async_computation.2 | async-start | bytes 1048576 | tf_op jit(solution)/shard_map/all_to_all | solution.py:82
  165.3 14.8 %collective-permute-start.1 = (f32[1024,128]{1,0:T(8,128)S(1)}, f32[1024,128]{1,0:T(8,128)S(1)}, u32[]{:S(2)}, u32[]{:S(2)}) collective-permute-start(f32[1024,128]{1,0:T(8,128)S(1)} %bitcast.145), channel_id=1, source_target_pairs={{0,8},{4,12},{8,0},{12,4},{16,24},{20,28},{24,16},{28,20},{32,40},... | collective-permute-start | bytes 1572872 | tf_op jit(solution)/shard_map/ppermute | solution.py:12
  186.0 11.5 %all-to-all-start.3 = ((f32[4,256,128]{2,1,0:T(8,128)}), f32[4,256,128]{2,1,0:T(8,128)S(1)}, u32[]{:S(2)}, u32[]{:S(2)}) async-start(f32[4,256,128]{2,1,0:T(8,128)} %stack.13), calls=%async_computation.3 | async-start | bytes 1048576 | tf_op jit(solution)/shard_map/all_to_all | solution.py:82
  197.5 24.9 %collective-permute-start.2 = (f32[1024,128]{1,0:T(8,128)S(1)}, f32[1024,128]{1,0:T(8,128)S(1)}, u32[]{:S(2)}, u32[]{:S(2)}) collective-permute-start(f32[1024,128]{1,0:T(8,128)S(1)} %bitcast.142), channel_id=1, source_target_pairs={{0,16},{4,20},{8,24},{12,28},{16,0},{20,4},{24,8},{28,12},{32,48},... | collective-permute-start | bytes 1572872 | tf_op jit(solution)/shard_map/ppermute | solution.py:12
  228.3 12.3 %all-to-all-start.4 = ((f32[4,256,128]{2,1,0:T(8,128)}), f32[4,256,128]{2,1,0:T(8,128)S(1)}, u32[]{:S(2)}, u32[]{:S(2)}) async-start(f32[4,256,128]{2,1,0:T(8,128)} %stack.14), calls=%async_computation.4 | async-start | bytes 1048576 | tf_op jit(solution)/shard_map/all_to_all | solution.py:82
  240.6 50.1 %collective-permute-start.3 = (f32[1024,128]{1,0:T(8,128)S(1)}, f32[1024,128]{1,0:T(8,128)S(1)}, u32[]{:S(2)}, u32[]{:S(2)}) collective-permute-start(f32[1024,128]{1,0:T(8,128)S(1)} %bitcast.146), channel_id=1, source_target_pairs={{0,32},{4,36},{8,40},{12,44},{16,48},{20,52},{24,56},{28,60},{32,0... | collective-permute-start | bytes 1572872 | tf_op jit(solution)/shard_map/ppermute | solution.py:12
  296.7 13.4 %all-to-all-start.5 = ((f32[4,256,128]{2,1,0:T(8,128)}), f32[4,256,128]{2,1,0:T(8,128)S(1)}, u32[]{:S(2)}, u32[]{:S(2)}) async-start(f32[4,256,128]{2,1,0:T(8,128)} %stack.15), calls=%async_computation.5 | async-start | bytes 1048576 | tf_op jit(solution)/shard_map/all_to_all | solution.py:82
  310.1 48.7 %collective-permute-start.4 = (f32[1024,128]{1,0:T(8,128)S(1)}, f32[1024,128]{1,0:T(8,128)S(1)}, u32[]{:S(2)}, u32[]{:S(2)}) collective-permute-start(f32[1024,128]{1,0:T(8,128)S(1)} %bitcast.144), channel_id=1, source_target_pairs={{0,64},{4,68},{8,72},{12,76},{16,80},{20,84},{24,88},{28,92},{32,9... | collective-permute-start | bytes 1572872 | tf_op jit(solution)/shard_map/ppermute | solution.py:12
  364.7 13.4 %all-to-all-start.6 = ((f32[4,256,128]{2,1,0:T(8,128)}), f32[4,256,128]{2,1,0:T(8,128)S(1)}, u32[]{:S(2)}, u32[]{:S(2)}) async-start(f32[4,256,128]{2,1,0:T(8,128)} %stack.16), calls=%async_computation.6 | async-start | bytes 1048576 | tf_op jit(solution)/shard_map/all_to_all | solution.py:82
  378.1 14.9 %collective-permute-start.5 = (f32[1024,128]{1,0:T(8,128)S(1)}, f32[1024,128]{1,0:T(8,128)S(1)}, u32[]{:S(2)}, u32[]{:S(2)}) collective-permute-start(f32[1024,128]{1,0:T(8,128)S(1)} %bitcast.143), channel_id=1, source_target_pairs={{0,128},{4,132},{8,136},{12,140},{16,144},{20,148},{24,152},{28,15... | collective-permute-start | bytes 1572872 | tf_op jit(solution)/shard_map/ppermute | solution.py:12
  398.9 11.6 %all-to-all-start.7 = ((f32[4,256,128]{2,1,0:T(8,128)}), f32[4,256,128]{2,1,0:T(8,128)S(1)}, u32[]{:S(2)}, u32[]{:S(2)}) async-start(f32[4,256,128]{2,1,0:T(8,128)} %stack.17), calls=%async_computation.7 | async-start | bytes 1048576 | tf_op jit(solution)/shard_map/all_to_all | solution.py:82
  410.5 14.3 %collective-permute-start.6 = (f32[1024,128]{1,0:T(8,128)S(1)}, f32[1024,128]{1,0:T(8,128)S(1)}, u32[]{:S(2)}, u32[]{:S(2)}) collective-permute-start(f32[1024,128]{1,0:T(8,128)S(1)} %bitcast.141), channel_id=1, source_target_pairs={{0,256},{4,260},{8,264},{12,268},{16,272},{20,276},{24,280},{28,28... | collective-permute-start | bytes 1572872 | tf_op jit(solution)/shard_map/ppermute | solution.py:12
Sparse Core Ops, SparseCore 0:
  91.0 49.8 all-reduce.1
